TPU v7x, 512 devices: a whole 4x8x8 slice. The times are simulated.
512 devices in a mesh: req: 64 (over x, z, core), tp: 8 (over y).
Axes of the slice: x: 4, y: 8, z: 8, core: 2. Of those that a mesh axis runs over, the one named last changes fastest.
Arguments:
- residual_input: bfloat16 [8192, 3584], P('req', 'tp'), may hold values from -6 to 6
- new_token_queries: bfloat16 [8192, 4096], P('req', 'tp'), may hold values from -8 to 8
- new_token_keys: bfloat16 [8192, 2048], P('req', 'tp'), may hold values from -8 to 8
- new_token_values: bfloat16 [8192, 2048], P('req', 'tp'), may hold values from -6 to 6
- key_page_pool: bfloat16 [1536, 16, 2048], P('req', None, 'tp'), may hold values from -6 to 6
- value_page_pool: bfloat16 [1536, 16, 2048], P('req', None, 'tp'), may hold values from -6 to 6
- request_page_table: int32 [128, 64], P('req'), may hold values from -1 to 23, as said below
- page_token_length: int32 [128, 64], P('req'), may hold values from 0 to 16, as said below
- request_token_length: int32 [64, 2], P('req'), may hold values from 1 to 96, 128 in all within a row
- request_adapter: int32 [64, 2], P('req'), may hold values from 0 to 63
- adapter_table_row: int32 [64], replicated, may hold values from 0 to 63, each once
- output_weight: bfloat16 [4096, 3584], P('tp'), may hold values from -0.125 to 0.125
- adapter_down_weight: bfloat16 [64, 16, 4096], P('req', None, 'tp'), may hold values from -0.09375 to 0.09375
- adapter_up_weight: bfloat16 [64, 16, 3584], P('req', None, 'tp'), may hold values from -1.5 to 1.5
- norm_scale_row: float32 [3584], P('tp'), may hold values from 0.25 to 1.75
Outputs:
- hidden_out: bfloat16 [8192, 3584], P('req', 'tp')
Inputs may be any that keep to these rules, and one draw needn't show every extreme that they name: request_page_table[q, o] is a page of the pool of owner o (rows o * 24 to o * 24 + 23 of the pools), or -1; so the 2 requests of one index of req take at most 2 pages from one owner, and in every draw the requests of some index of req each take a page from every owner. Requests may share pages. `page_token_length`: 0 exactly where request_page_table is -1; every used page of a request is full but at most one.
All inputs are finite; a program needn't handle non-finite values.
Results may differ from a plain program's by a relative error of at most 0.015.
Values may be sent and summed in bfloat16 or wider, within the bound.
No kernel may reach another device: no remote copies, remote signals or barrier semaphores. Data moves between devices by JAX's collectives and lax.ppermute only.
A program may use at most 64 MiB of HBM per device.

v0:
```python
import jax
import jax.numpy as jnp
from jax import lax
from jax.sharding import PartitionSpec as P

HEAD_SIZE = 256
epsilon = 1e-06
adapter_scale = 2.0
masked_score = -1e30


def attend(query_rows, new_keys, new_values, gathered_keys, gathered_values, usable, owner_request):
    token_count = query_rows.shape[0]
    kv_heads = new_keys.shape[1] // HEAD_SIZE
    group_size = query_rows.shape[1] // new_keys.shape[1]
    requests_here = gathered_keys.shape[0]
    cached_count = gathered_keys.shape[1]
    query_heads = query_rows.reshape(token_count, kv_heads, group_size, HEAD_SIZE)
    past_keys = gathered_keys.reshape(requests_here, cached_count, kv_heads, HEAD_SIZE)
    past_values = gathered_values.reshape(requests_here * cached_count, kv_heads, HEAD_SIZE)
    fresh_keys = new_keys.reshape(token_count, kv_heads, HEAD_SIZE)
    fresh_values = new_values.reshape(token_count, kv_heads, HEAD_SIZE)
    positions = jnp.arange(token_count, dtype=jnp.int32)
    scaling = HEAD_SIZE ** (-0.5)
    past_scores = (
        jnp.einsum("tgqd,rngd->tgqrn", query_heads, past_keys, preferred_element_type=jnp.float32)
        * scaling
    )
    past_mask = usable[None, :, :] & (
        owner_request[:, None, None] == jnp.arange(requests_here, dtype=jnp.int32)[None, :, None]
    )
    past_scores = jnp.where(past_mask[:, None, None, :, :], past_scores, masked_score)
    past_scores = past_scores.reshape(
        token_count, kv_heads, group_size, requests_here * cached_count
    )
    fresh_scores = (
        jnp.einsum("tgqd,ugd->tgqu", query_heads, fresh_keys, preferred_element_type=jnp.float32)
        * scaling
    )
    fresh_mask = (owner_request[:, None] == owner_request[None, :]) & (
        positions[None, :] <= positions[:, None]
    )
    fresh_scores = jnp.where(fresh_mask[:, None, None, :], fresh_scores, masked_score)
    scores = jnp.concatenate([past_scores, fresh_scores], axis=3)
    highest = jnp.max(scores, axis=3, keepdims=True)
    weights = jnp.exp(scores - highest)
    weights = (weights / jnp.sum(weights, axis=3, keepdims=True)).astype(jnp.bfloat16)
    all_values = jnp.concatenate([past_values, fresh_values], axis=0)
    mixed = jnp.einsum("tgqk,kgd->tgqd", weights, all_values, preferred_element_type=jnp.float32)
    return mixed.reshape(token_count, -1).astype(jnp.bfloat16)


def local(
    residual_input,
    new_token_queries,
    new_token_keys,
    new_token_values,
    key_page_pool,
    value_page_pool,
    request_page_table,
    page_token_length,
    request_token_length,
    request_adapter,
    adapter_table_row,
    output_weight,
    adapter_down_weight,
    adapter_up_weight,
    norm_scale_row,
):
    owners = lax.axis_size("req")
    groups = lax.axis_size("tp")
    requests_here = request_page_table.shape[0]
    page_rows = key_page_pool.shape[1]
    token_count = new_token_queries.shape[0]
    width_part = residual_input.shape[1]
    head_cols = key_page_pool.shape[2]
    down_cols = adapter_down_weight.shape[2]
    adapter_pair = jnp.concatenate([adapter_down_weight, adapter_up_weight], axis=2)
    adapters_everywhere = lax.all_gather(adapter_pair, "req", axis=0, tiled=True)
    wanted = lax.all_to_all(request_page_table, "req", split_axis=1, concat_axis=1, tiled=True)
    page_picks = jnp.maximum(wanted, 0)
    kv_pool = jnp.concatenate([key_page_pool, value_page_pool], axis=2)
    kv_out = kv_pool[page_picks]
    kv_back = lax.all_to_all(kv_out, "req", split_axis=1, concat_axis=1, tiled=True)
    kv_back = kv_back.reshape(requests_here, owners * page_rows, 2 * head_cols)
    gathered_keys = kv_back[:, :, :head_cols]
    gathered_values = kv_back[:, :, head_cols:]
    usable = (
        jnp.arange(page_rows, dtype=jnp.int32)[None, None, :] < page_token_length[:, :, None]
    ).reshape(requests_here, owners * page_rows)
    lengths = request_token_length[0]
    positions = jnp.arange(token_count, dtype=jnp.int32)
    ends = jnp.cumsum(lengths)
    owner_request = jnp.sum((positions[:, None] >= ends[None, :]).astype(jnp.int32), axis=1)
    attention = attend(
        new_token_queries,
        new_token_keys,
        new_token_values,
        gathered_keys,
        gathered_values,
        usable,
        owner_request,
    )
    adapters_all = adapter_table_row.shape[0]
    matches = request_adapter[0][:, None] == jnp.arange(adapters_all, dtype=jnp.int32)[None, :]
    chosen_pages = jnp.sum(jnp.where(matches, adapter_table_row[None, :], 0), axis=1)
    rows_here = adapters_everywhere.shape[0]
    picker = (chosen_pages[:, None] == jnp.arange(rows_here, dtype=jnp.int32)[None, :]).astype(
        jnp.bfloat16
    )
    selected = jnp.einsum(
        "rk,kab->rab", picker, adapters_everywhere, preferred_element_type=jnp.float32
    ).astype(jnp.bfloat16)
    adapter_in = selected[:, :, :down_cols]
    adapter_out = selected[:, :, down_cols:]
    rank_size = adapter_in.shape[1]
    selector = (
        owner_request[:, None] == jnp.arange(requests_here, dtype=jnp.int32)[None, :]
    ).astype(jnp.float32)
    selector_half = selector.astype(jnp.bfloat16)
    base_part = jnp.dot(attention, output_weight, preferred_element_type=jnp.float32)
    low_terms = jnp.einsum("tc,rkc->trk", attention, adapter_in, preferred_element_type=jnp.float32)
    low_part = jnp.sum(low_terms * selector[:, :, None], axis=1)
    base_slots = base_part.astype(jnp.bfloat16).reshape(token_count, groups, width_part)
    base_slots = jnp.transpose(base_slots, (1, 0, 2))
    low_slots = jnp.broadcast_to(
        low_part.astype(jnp.bfloat16)[None], (groups, token_count, rank_size)
    )
    pad_cols = -(width_part + rank_size) % 128
    slots = jnp.concatenate(
        [base_slots, low_slots, jnp.zeros((groups, token_count, pad_cols), jnp.bfloat16)], axis=2
    )
    arrived = lax.all_to_all(slots, "tp", split_axis=0, concat_axis=0, tiled=True)
    arrived = arrived.astype(jnp.float32)
    base_local = jnp.sum(arrived[:, :, :width_part], axis=0)
    low_sum = jnp.sum(arrived[:, :, width_part : width_part + rank_size], axis=0)
    rows_masked = (low_sum.astype(jnp.bfloat16)[:, None, :] * selector_half[:, :, None]).reshape(
        token_count, requests_here * rank_size
    )
    projected = base_local + adapter_scale * jnp.dot(
        rows_masked,
        adapter_out.reshape(requests_here * rank_size, width_part),
        preferred_element_type=jnp.float32,
    )
    square_part = jnp.sum(projected * projected, axis=1)
    square_sum = lax.psum(square_part, "tp")
    mean_square = square_sum / (groups * width_part)
    scaled = projected * lax.rsqrt(mean_square + epsilon)[:, None]
    return (residual_input.astype(jnp.float32) + scaled * norm_scale_row).astype(jnp.bfloat16)


def solution(mesh):
    in_specs = (
        P("req", "tp"),
        P("req", "tp"),
        P("req", "tp"),
        P("req", "tp"),
        P("req", None, "tp"),
        P("req", None, "tp"),
        P("req", None),
        P("req", None),
        P("req", None),
        P("req", None),
        P(),
        P("tp", None),
        P("req", None, "tp"),
        P("req", None, "tp"),
        P("tp"),
    )
    out_specs = P("req", "tp")
    return jax.shard_map(local, mesh=mesh, in_specs=in_specs, out_specs=out_specs, check_vma=False)
```

profile of v0, /device:TPU:8, one launch (start us, length us, event | category | flops | bytes accessed | tf_op | source)
XLA Modules:
  0.0 186.8 jit_solution(3870955451242989684)
XLA Ops:
  6.5 1.4 copy.88
  8.0 13.8 %all-to-all-start = ((s32[2,64,1]{0,2,1:T(1,128)}), s32[2,64,1]{0,2,1:T(1,128)S(1)}, u32[]{:S(2)}, u32[]{:S(2)}) async-start(s32[2,64,1]{0,2,1:T(1,128)} %copy.88), calls=%async_computation | async-start | bytes 65536 | tf_op jit(solution)/shard_map/all_to_all | solution.py:80
  21.8 1.4 pad_maximum_fusion.1
  23.2 1.1 pad_maximum_fusion
  24.2 7.0 %all-to-all-done = s32[2,64,1]{0,2,1:T(1,128)S(1)} async-done(((s32[2,64,1]{0,2,1:T(1,128)}), s32[2,64,1]{0,2,1:T(1,128)S(1)}, u32[]{:S(2)}, u32[]{:S(2)}) %all-to-all-start) | async-done | bytes 544 | tf_op jit(solution)/shard_map/all_to_all | solution.py:80
  31.4 0.7 gather_fusion
  32.1 1.6 copy.90
  33.7 4.8 %all-to-all-start.1 = ((bf16[2,64,16,512]{3,2,0,1:T(8,128)(2,1)}), bf16[2,64,16,512]{3,2,0,1:T(8,128)(2,1)S(1)}, u32[]{:S(2)}, u32[]{:S(2)}) async-start(bf16[2,64,16,512]{3,2,0,1:T(8,128)(2,1)} %copy.90), calls=%async_computation.1 | async-start | bytes 4194304 | tf_op jit(solution)/shard_map/all_to_all | solution.py:84
  38.5 0.7 copy.92
  40.6 0.9 fusion.38
  41.4 71.5 %all-gather.2.cloned.1.call-done = bf16[64,16,960]{2,1,0:T(8,128)(2,1)} async-done(((bf16[1,16,960]{2,1,0:T(8,128)(2,1)}), bf16[64,16,960]{2,1,0:T(8,128)(2,1)}) %all-gather.2.cloned.1.call-update) | async-done | bytes 1966096 | tf_op jit(solution)/shard_map/all_gather | solution.py:79
  112.9 3.9 %fusion.10 = bf16[2,16,960]{2,0,1:T(2,128)(2,1)S(1)} fusion(bf16[64,16,960]{2,1,0:T(8,128)(2,1)} %all-gather.2.cloned.1.call-done, s32[2]{0:T(128)S(1)} %fusion.31), kind=kOutput, calls=%fused_computation.19 | convolution fusion | flops 3963008 | bytes 2027528 | tf_op jit(solution)/shard_map/rk,kab->rab/dot_general | solution.py:111
  117.4 1.3 copy-done.1
  118.9 1.4 copy.93
  120.8 1.4 fusion.37
  122.5 0.7 copy-done.6
  124.2 1.5 copy-done.3
  125.7 0.7 convolution_convert_fusion
  126.4 0.6 copy.99
  127.2 1.3 maximum_maximum_fusion
  128.4 6.8 %all-to-all-start.2 = ((bf16[8,128,512]{1,2,0:T(8,128)(2,1)}), bf16[8,128,512]{1,2,0:T(8,128)(2,1)S(1)}, u32[]{:S(2)}, u32[]{:S(2)}) async-start(bf16[8,128,512]{1,2,0:T(8,128)(2,1)} %maximum_maximum_fusion), calls=%async_computation.2 | async-start | bytes 2097152 | tf_op jit(solution)/shard_map/all_to_all | solution.py:133
  135.3 27.7 %all-to-all-done.2 = bf16[8,128,512]{1,2,0:T(8,128)(2,1)S(1)} async-done(((bf16[8,128,512]{1,2,0:T(8,128)(2,1)}), bf16[8,128,512]{1,2,0:T(8,128)(2,1)S(1)}, u32[]{:S(2)}, u32[]{:S(2)}) %all-to-all-start.2) | async-done | bytes 1048608 | tf_op jit(solution)/shard_map/all_to_all | solution.py:133
  163.5 15.6 %psum.7 = f32[128]{0:T(128)S(1)} all-reduce(f32[128]{0:T(128)S(1)} %get-tuple-element.12), channel_id=1, replica_groups=mesh['req'=64,'tp'=8] {'tp'}, use_global_device_ids=true, to_apply=%region_10.11 | all-reduce | flops 128 | bytes 1024 | tf_op jit(solution)/shard_map/psum | solution.py:146
  179.1 0.8 add_convert_fusion
  (66 shorter events, 4.6 us)
Async XLA Ops:
  6.5 34.0 %copy-start = (bf16[128,256]{1,0:T(8,128)(2,1)S(1)}, bf16[128,256]{1,0:T(8,128)(2,1)}, u32[]{:S(2)}) copy-start(bf16[128,256]{1,0:T(8,128)(2,1)} %param.17) | copy-start | bytes 196612
  8.0 23.2 %all-to-all-start = ((s32[2,64,1]{0,2,1:T(1,128)}), s32[2,64,1]{0,2,1:T(1,128)S(1)}, u32[]{:S(2)}, u32[]{:S(2)}) async-start(s32[2,64,1]{0,2,1:T(1,128)} %copy.88), calls=%async_computation | async-start | bytes 65536 | tf_op jit(solution)/shard_map/all_to_all | solution.py:80
  21.7 91.2 %all-gather.2.cloned.1.call-start = ((), (), s32[]{:S(2)}) async-start(), calls=%async_computation.3 | async-start | bytes 2129920 | tf_op jit(solution)/shard_map/all_gather | solution.py:79
  33.7 4.9 %copy-start.8 = (bf16[128,256]{1,0:T(8,128)(2,1)S(1)}, bf16[128,256]{1,0:T(8,128)(2,1)}, u32[]{:S(2)}) copy-start(bf16[128,256]{1,0:T(8,128)(2,1)} %param.18) | copy-start | bytes 196612
  33.7 5.6 %copy-start.11 = (s32[2,64]{1,0:T(2,128)S(1)}, s32[2,64]{1,0:T(2,128)}, u32[]{:S(2)}) copy-start(s32[2,64]{1,0:T(2,128)} %param.22) | copy-start | bytes 1540
  33.7 5.9 %copy-start.13 = (s32[1,2]{1,0:T(1,128)S(1)}, s32[1,2]{1,0:T(1,128)}, u32[]{:S(2)}) copy-start(s32[1,2]{1,0:T(1,128)} %param.23) | copy-start | bytes 28
  33.7 6.2 %copy-start.14 = (s32[64]{0:T(128)S(1)}, s32[64]{0:T(128)}, u32[]{:S(2)}) copy-start(s32[64]{0:T(128)} %param.25) | copy-start | bytes 772
  33.7 6.2 %copy-start.15 = (s32[1,2]{1,0:T(1,128)S(1)}, s32[1,2]{1,0:T(1,128)}, u32[]{:S(2)}) copy-start(s32[1,2]{1,0:T(1,128)} %param.24) | copy-start | bytes 28
  33.7 6.9 %copy-start.12 = (bf16[128,512]{1,0:T(8,128)(2,1)S(1)}, bf16[128,512]{1,0:T(8,128)(2,1)}, u32[]{:S(2)}) copy-start(bf16[128,512]{1,0:T(8,128)(2,1)} %param.16) | copy-start | bytes 393220
  33.7 83.1 %all-to-all-start.1 = ((bf16[2,64,16,512]{3,2,0,1:T(8,128)(2,1)}), bf16[2,64,16,512]{3,2,0,1:T(8,128)(2,1)S(1)}, u32[]{:S(2)}, u32[]{:S(2)}) async-start(bf16[2,64,16,512]{3,2,0,1:T(8,128)(2,1)} %copy.90), calls=%async_computation.1 | async-start | bytes 4194304 | tf_op jit(solution)/shard_map/all_to_all | solution.py:84
  116.8 0.6 copy-start.5
  117.4 1.3 copy-start.1
  118.8 2.0 %copy-start.2 = (bf16[2,64,16,512]{3,2,1,0:T(8,128)(2,1)S(1)}, bf16[2,64,16,512]{3,2,1,0:T(8,128)(2,1)}, u32[]{:S(2)}) copy-start(bf16[2,64,16,512]{3,2,1,0:T(8,128)(2,1)} %copy-done.1) | copy-start | bytes 6291460
  122.3 0.9 copy-start.6
  122.4 1.2 copy-start.4
  122.4 1.2 copy-start.9
  123.7 2.0 %copy-start.3 = (bf16[512,3584]{1,0:T(8,128)(2,1)S(1)}, bf16[512,3584]{1,0:T(8,128)(2,1)}, u32[]{:S(2)}) copy-start(bf16[512,3584]{1,0:T(8,128)(2,1)} %param.26) | copy-start | bytes 11010052
  125.7 1.3 slice-start
  128.4 34.5 %all-to-all-start.2 = ((bf16[8,128,512]{1,2,0:T(8,128)(2,1)}), bf16[8,128,512]{1,2,0:T(8,128)(2,1)S(1)}, u32[]{:S(2)}, u32[]{:S(2)}) async-start(bf16[8,128,512]{1,2,0:T(8,128)(2,1)} %maximum_maximum_fusion), calls=%async_computation.2 | async-start | bytes 2097152 | tf_op jit(solution)/shard_map/all_to_all | solution.py:133
  135.3 27.9 %slice-start.1 = ((bf16[2,16,960]{2,0,1:T(2,128)(2,1)}), bf16[2,16,448]{2,0,1:T(2,128)(2,1)S(1)}, s32[]{:S(2)}) async-start(bf16[2,16,960]{2,0,1:T(2,128)(2,1)} %copy-done.5), calls=%async_computation.5 | async-start | bytes 65536 | tf_op jit(solution)/shard_map/slice | solution.py:115
  163.1 16.1 %copy-start.7 = (bf16[128,448]{0,1:T(8,128)(2,1)S(1)}, bf16[128,448]{0,1:T(8,128)(2,1)}, u32[]{:S(2)}) copy-start(bf16[128,448]{0,1:T(8,128)(2,1)} %param.15) | copy-start | bytes 344068
  163.1 16.1 %copy-start.10 = (f32[448]{0:T(512)S(1)}, f32[448]{0:T(512)}, u32[]{:S(2)}) copy-start(f32[448]{0:T(512)} %param.29) | copy-start | bytes 5380
Sparse Core Ops, SparseCore 0:
  25.9 86.9 all-gather.1
where the time goes:
time: 187 us
  waiting for transfers between devices  106 us (57%)
  starting transfers between devices  25.5 us (14%)
  blocking collectives  15.6 us (8%)
  between operations  13.7 us (7%)
  local copies, waits for them, and re-layouts  12.1 us (6%)
  matrix products  7.86 us (4%)
  other arithmetic  5.9 us (3%)
    all_gather x1, waiting for transfers between devices, local(): lax.all_gather(adapter_pair, 'req', axis=0, tiled=True)  71.5 us
    all_to_all x1, waiting for transfers between devices, local(): lax.all_to_all(slots, 'tp', split_axis=0, concat_axis=0, tiled=True)  27.7 us
    psum x1, blocking collectives, local(): square_sum = lax.psum(square_part, 'tp')  15.6 us
    all_to_all x1, starting transfers between devices, local(): lax.all_to_all(request_page_table, 'req', split_axis=1, concat_axis=1, ti...  13.8 us
    all_to_all x1, waiting for transfers between devices, local(): lax.all_to_all(request_page_table, 'req', split_axis=1, concat_axis=1, ti...  6.97 us
    all_to_all x1, starting transfers between devices, local(): lax.all_to_all(slots, 'tp', split_axis=0, concat_axis=0, tiled=True)  6.83 us
    unnamed x33, local copies, waits for them, and re-layouts  5.44 us
    all_to_all x1, starting transfers between devices, local(): lax.all_to_all(kv_out, 'req', split_axis=1, concat_axis=1, tiled=True)  4.84 us
  transfers between devices with their start and end apart: 4, of which 3 were waited for; matrix products, arithmetic and copies ran while one was open for 6% of the time, Pallas kernels for 0%

commit v1 on v0

--- a/solution.py
+++ b/solution.py
@@ -143,7 +143,7 @@
         preferred_element_type=jnp.float32,
     )
     square_part = jnp.sum(projected * projected, axis=1)
-    square_sum = lax.psum(square_part, "tp")
+    square_sum = jnp.sum(lax.all_gather(square_part, "tp"), axis=0)
     mean_square = square_sum / (groups * width_part)
     scaled = projected * lax.rsqrt(mean_square + epsilon)[:, None]
     return (residual_input.astype(jnp.float32) + scaled * norm_scale_row).astype(jnp.bfloat16)

time: 187 us -> 187 us (level)
    psum x1 -> x0, blocking collectives: 15.6 us -> none  [local(): square_sum = lax.psum(square_part, 'tp')]
    all_gather x0 -> x1, blocking collectives: none -> 14.8 us  [local(): square_sum = jnp.sum(lax.all_gather(square_part, 'tp'), axis=0)]
where the time goes in v1:
time: 187 us; the launch traced here: 186 us
  waiting for transfers between devices  106 us (57%)
  starting transfers between devices  25.5 us (14%)
  blocking collectives  14.8 us (8%)
  between operations  13.7 us (7%)
  local copies, waits for them, and re-layouts  12.1 us (6%)
  matrix products  7.86 us (4%)
  other arithmetic  5.92 us (3%)
    all_gather x1, waiting for transfers between devices, local(): lax.all_gather(adapter_pair, 'req', axis=0, tiled=True)  71.5 us
    all_to_all x1, waiting for transfers between devices, local(): lax.all_to_all(slots, 'tp', split_axis=0, concat_axis=0, tiled=True)  27.7 us
    all_gather x1, blocking collectives, local(): square_sum = jnp.sum(lax.all_gather(square_part, 'tp'), axis=0)  14.8 us
    all_to_all x1, starting transfers between devices, local(): lax.all_to_all(request_page_table, 'req', split_axis=1, concat_axis=1, ti...  13.8 us
    all_to_all x1, waiting for transfers between devices, local(): lax.all_to_all(request_page_table, 'req', split_axis=1, concat_axis=1, ti...  6.97 us
    all_to_all x1, starting transfers between devices, local(): lax.all_to_all(slots, 'tp', split_axis=0, concat_axis=0, tiled=True)  6.83 us
    unnamed x33, local copies, waits for them, and re-layouts  5.44 us
    all_to_all x1, starting transfers between devices, local(): lax.all_to_all(kv_out, 'req', split_axis=1, concat_axis=1, tiled=True)  4.84 us
  transfers between devices with their start and end apart: 4, of which 3 were waited for; matrix products, arithmetic and copies ran while one was open for 6% of the time, Pallas kernels for 0%

profile of v1, /device:TPU:8, one launch (start us, length us, event | category | flops | bytes accessed | tf_op | source)
XLA Modules:
  0.0 185.9 jit_solution(15272181103660975062)
XLA Ops:
  6.5 1.4 copy.88
  8.0 13.8 %all-to-all-start = ((s32[2,64,1]{0,2,1:T(1,128)}), s32[2,64,1]{0,2,1:T(1,128)S(1)}, u32[]{:S(2)}, u32[]{:S(2)}) async-start(s32[2,64,1]{0,2,1:T(1,128)} %copy.88), calls=%async_computation | async-start | bytes 65536 | tf_op jit(solution)/shard_map/all_to_all | solution.py:80
  21.8 1.4 pad_maximum_fusion.1
  23.2 1.1 pad_maximum_fusion
  24.2 7.0 %all-to-all-done = s32[2,64,1]{0,2,1:T(1,128)S(1)} async-done(((s32[2,64,1]{0,2,1:T(1,128)}), s32[2,64,1]{0,2,1:T(1,128)S(1)}, u32[]{:S(2)}, u32[]{:S(2)}) %all-to-all-start) | async-done | bytes 544 | tf_op jit(solution)/shard_map/all_to_all | solution.py:80
  31.4 0.7 gather_fusion
  32.1 1.6 copy.90
  33.7 4.8 %all-to-all-start.1 = ((bf16[2,64,16,512]{3,2,0,1:T(8,128)(2,1)}), bf16[2,64,16,512]{3,2,0,1:T(8,128)(2,1)S(1)}, u32[]{:S(2)}, u32[]{:S(2)}) async-start(bf16[2,64,16,512]{3,2,0,1:T(8,128)(2,1)} %copy.90), calls=%async_computation.1 | async-start | bytes 4194304 | tf_op jit(solution)/shard_map/all_to_all | solution.py:84
  38.5 0.7 copy.92
  40.6 0.9 fusion.38
  41.4 71.5 %all-gather.4.cloned.1.call-done = bf16[64,16,960]{2,1,0:T(8,128)(2,1)} async-done(((bf16[1,16,960]{2,1,0:T(8,128)(2,1)}), bf16[64,16,960]{2,1,0:T(8,128)(2,1)}) %all-gather.4.cloned.1.call-update) | async-done | bytes 1966096 | tf_op jit(solution)/shard_map/all_gather | solution.py:79
  112.9 3.9 %fusion.10 = bf16[2,16,960]{2,0,1:T(2,128)(2,1)S(1)} fusion(bf16[64,16,960]{2,1,0:T(8,128)(2,1)} %all-gather.4.cloned.1.call-done, s32[2]{0:T(128)S(1)} %fusion.31), kind=kOutput, calls=%fused_computation.19 | convolution fusion | flops 3963008 | bytes 2027528 | tf_op jit(solution)/shard_map/rk,kab->rab/dot_general | solution.py:111
  117.4 1.3 copy-done.1
  118.9 1.4 copy.93
  120.8 1.4 fusion.37
  122.5 0.7 copy-done.6
  124.2 1.5 copy-done.3
  125.7 0.7 convolution_convert_fusion
  126.4 0.6 copy.99
  127.2 1.3 maximum_maximum_fusion
  128.4 6.8 %all-to-all-start.2 = ((bf16[8,128,512]{1,2,0:T(8,128)(2,1)}), bf16[8,128,512]{1,2,0:T(8,128)(2,1)S(1)}, u32[]{:S(2)}, u32[]{:S(2)}) async-start(bf16[8,128,512]{1,2,0:T(8,128)(2,1)} %maximum_maximum_fusion), calls=%async_computation.2 | async-start | bytes 2097152 | tf_op jit(solution)/shard_map/all_to_all | solution.py:133
  135.3 27.7 %all-to-all-done.2 = bf16[8,128,512]{1,2,0:T(8,128)(2,1)S(1)} async-done(((bf16[8,128,512]{1,2,0:T(8,128)(2,1)}), bf16[8,128,512]{1,2,0:T(8,128)(2,1)S(1)}, u32[]{:S(2)}, u32[]{:S(2)}) %all-to-all-start.2) | async-done | bytes 1048608 | tf_op jit(solution)/shard_map/all_to_all | solution.py:133
  163.5 14.8 %all-gather.1 = f32[8,1,128]{2,1,0:T(1,128)S(1)} all-gather(f32[1,1,128]{2,1,0:T(1,128)S(1)} %bitcast.88), channel_id=2, replica_groups=mesh['req'=64,'tp'=8] {'tp'}, dimensions={0}, use_global_device_ids=true | all-gather | bytes 4608 | tf_op jit(solution)/shard_map/all_gather | solution.py:146
  178.3 0.8 add_convert_fusion
  (67 shorter events, 4.6 us)
Async XLA Ops:
  6.5 34.0 %copy-start = (bf16[128,256]{1,0:T(8,128)(2,1)S(1)}, bf16[128,256]{1,0:T(8,128)(2,1)}, u32[]{:S(2)}) copy-start(bf16[128,256]{1,0:T(8,128)(2,1)} %param.17) | copy-start | bytes 196612
  8.0 23.2 %all-to-all-start = ((s32[2,64,1]{0,2,1:T(1,128)}), s32[2,64,1]{0,2,1:T(1,128)S(1)}, u32[]{:S(2)}, u32[]{:S(2)}) async-start(s32[2,64,1]{0,2,1:T(1,128)} %copy.88), calls=%async_computation | async-start | bytes 65536 | tf_op jit(solution)/shard_map/all_to_all | solution.py:80
  21.7 91.2 %all-gather.4.cloned.1.call-start = ((), (), s32[]{:S(2)}) async-start(), calls=%async_computation.3 | async-start | bytes 2129920 | tf_op jit(solution)/shard_map/all_gather | solution.py:79
  33.7 4.9 %copy-start.8 = (bf16[128,256]{1,0:T(8,128)(2,1)S(1)}, bf16[128,256]{1,0:T(8,128)(2,1)}, u32[]{:S(2)}) copy-start(bf16[128,256]{1,0:T(8,128)(2,1)} %param.18) | copy-start | bytes 196612
  33.7 5.6 %copy-start.11 = (s32[2,64]{1,0:T(2,128)S(1)}, s32[2,64]{1,0:T(2,128)}, u32[]{:S(2)}) copy-start(s32[2,64]{1,0:T(2,128)} %param.22) | copy-start | bytes 1540
  33.7 5.9 %copy-start.13 = (s32[1,2]{1,0:T(1,128)S(1)}, s32[1,2]{1,0:T(1,128)}, u32[]{:S(2)}) copy-start(s32[1,2]{1,0:T(1,128)} %param.23) | copy-start | bytes 28
  33.7 6.2 %copy-start.14 = (s32[64]{0:T(128)S(1)}, s32[64]{0:T(128)}, u32[]{:S(2)}) copy-start(s32[64]{0:T(128)} %param.25) | copy-start | bytes 772
  33.7 6.2 %copy-start.15 = (s32[1,2]{1,0:T(1,128)S(1)}, s32[1,2]{1,0:T(1,128)}, u32[]{:S(2)}) copy-start(s32[1,2]{1,0:T(1,128)} %param.24) | copy-start | bytes 28
  33.7 6.9 %copy-start.12 = (bf16[128,512]{1,0:T(8,128)(2,1)S(1)}, bf16[128,512]{1,0:T(8,128)(2,1)}, u32[]{:S(2)}) copy-start(bf16[128,512]{1,0:T(8,128)(2,1)} %param.16) | copy-start | bytes 393220
  33.7 83.1 %all-to-all-start.1 = ((bf16[2,64,16,512]{3,2,0,1:T(8,128)(2,1)}), bf16[2,64,16,512]{3,2,0,1:T(8,128)(2,1)S(1)}, u32[]{:S(2)}, u32[]{:S(2)}) async-start(bf16[2,64,16,512]{3,2,0,1:T(8,128)(2,1)} %copy.90), calls=%async_computation.1 | async-start | bytes 4194304 | tf_op jit(solution)/shard_map/all_to_all | solution.py:84
  116.8 0.6 copy-start.5
  117.4 1.3 copy-start.1
  118.8 2.0 %copy-start.2 = (bf16[2,64,16,512]{3,2,1,0:T(8,128)(2,1)S(1)}, bf16[2,64,16,512]{3,2,1,0:T(8,128)(2,1)}, u32[]{:S(2)}) copy-start(bf16[2,64,16,512]{3,2,1,0:T(8,128)(2,1)} %copy-done.1) | copy-start | bytes 6291460
  122.3 0.9 copy-start.6
  122.4 1.2 copy-start.4
  122.4 1.2 copy-start.9
  123.7 2.0 %copy-start.3 = (bf16[512,3584]{1,0:T(8,128)(2,1)S(1)}, bf16[512,3584]{1,0:T(8,128)(2,1)}, u32[]{:S(2)}) copy-start(bf16[512,3584]{1,0:T(8,128)(2,1)} %param.26) | copy-start | bytes 11010052
  125.7 1.3 slice-start
  128.4 34.5 %all-to-all-start.2 = ((bf16[8,128,512]{1,2,0:T(8,128)(2,1)}), bf16[8,128,512]{1,2,0:T(8,128)(2,1)S(1)}, u32[]{:S(2)}, u32[]{:S(2)}) async-start(bf16[8,128,512]{1,2,0:T(8,128)(2,1)} %maximum_maximum_fusion), calls=%async_computation.2 | async-start | bytes 2097152 | tf_op jit(solution)/shard_map/all_to_all | solution.py:133
  135.3 27.9 %slice-start.1 = ((bf16[2,16,960]{2,0,1:T(2,128)(2,1)}), bf16[2,16,448]{2,0,1:T(2,128)(2,1)S(1)}, s32[]{:S(2)}) async-start(bf16[2,16,960]{2,0,1:T(2,128)(2,1)} %copy-done.5), calls=%async_computation.5 | async-start | bytes 65536 | tf_op jit(solution)/shard_map/slice | solution.py:115
  163.1 15.3 %copy-start.7 = (bf16[128,448]{0,1:T(8,128)(2,1)S(1)}, bf16[128,448]{0,1:T(8,128)(2,1)}, u32[]{:S(2)}) copy-start(bf16[128,448]{0,1:T(8,128)(2,1)} %param.15) | copy-start | bytes 344068
  163.1 15.2 %copy-start.10 = (f32[448]{0:T(512)S(1)}, f32[448]{0:T(512)}, u32[]{:S(2)}) copy-start(f32[448]{0:T(512)} %param.29) | copy-start | bytes 5380
Sparse Core Ops, SparseCore 0:
  25.9 86.9 all-gather.3
